TPU v7x, 512 devices: a whole 4x8x8 slice. The times are simulated.
512 devices in a mesh: section: 32 (over z, x), et: 16 (over y, core).
Axes of the slice: x: 4, y: 8, z: 8, core: 2. Of those that a mesh axis runs over, the one named last changes fastest.
Arguments:
- x_fwd: bfloat16 [32, 256, 3072], P('section', 'et'), may hold values from -6 to 6
- act_fwd: bfloat16 [32, 256, 8192], P('section', None, 'et'), may hold values from -6 to 6
- ids_fwd: int32 [32, 256, 2], P('section'), may hold values from 0 to 7, as said below
- x_bwd: bfloat16 [32, 256, 3072], P('section', 'et'), may hold values from -6 to 6
- act_bwd: bfloat16 [32, 256, 8192], P('section', None, 'et'), may hold values from -6 to 6
- ids_bwd: int32 [32, 256, 2], P('section'), may hold values from 0 to 7, as said below
- grad_out: bfloat16 [32, 256, 3072], P('section', 'et'), may hold values from -6 to 6
- gain: bfloat16 [32, 3072], P('section'), may hold values from 0.099609375 to 1.8984375
- w_router: bfloat16 [32, 3072, 8], P('section'), may hold values from -0.21875 to 0.21875
- w_down: bfloat16 [32, 8192, 3072], P('section', 'et'), may hold values from -0.0625 to 0.0625
Outputs:
- fwd_in: bfloat16 [32, 256, 3072], P('section', 'et')
- incoming_gradient: bfloat16 [32, 256, 3072], P('section', 'et')
- dact: bfloat16 [32, 256, 8192], P('section', None, 'et')
Inputs may be any that keep to these rules, and one draw needn't show every extreme that they name: `ids_fwd`: each token names 2 different experts; in each section's micro-batch exactly 128 tokens name expert 0. `ids_bwd`: each token names 2 different experts; in each section's micro-batch exactly 128 tokens name expert 0.
All inputs are finite; a program needn't handle non-finite values.
Results may differ from a plain program's by a relative error of at most 0.014.
Values may be sent and summed in bfloat16 or wider, within the bound.
No kernel may reach another device: no remote copies, remote signals or barrier semaphores. Data moves between devices by JAX's collectives and lax.ppermute only.
A program may use at most 64 MiB of HBM per device.

v0:
```python
import jax
import jax.numpy as jnp
from jax import lax
from jax.sharding import PartitionSpec as P


def from_behind(value, axis, steps):
    count = lax.axis_size(axis)
    first, last = (max(0, -steps), min(count, count - steps))
    return lax.ppermute(value, axis, [(source, source + steps) for source in range(first, last)])


def norm_logits(inputs, gain, w_router):
    wide = inputs.astype(jnp.float32)
    inverse = lax.rsqrt(jnp.mean(wide * wide, axis=-1, keepdims=True) + 1e-05)
    normed = (wide * inverse * gain.astype(jnp.float32)).astype(jnp.bfloat16)
    logits = jnp.dot(normed, w_router, preferred_element_type=jnp.float32).astype(jnp.bfloat16)
    return (wide, inverse, logits)


def routing(logits, chosen, experts):
    route = jnp.sum((chosen == 0).astype(jnp.float32), axis=1)
    partner = jnp.minimum(jnp.sum(chosen, axis=1), experts - 1)
    labels = jnp.arange(experts, dtype=jnp.int32)
    onehot = (partner[:, None] == labels[None, :]).astype(jnp.float32)
    wide_logits = logits.astype(jnp.float32)
    sigma = jax.nn.sigmoid(wide_logits[:, 0] - jnp.sum(wide_logits * onehot, axis=1))
    return (route, onehot, sigma, route * sigma)


def arrange(chosen):
    member = jnp.sum((chosen == 0).astype(jnp.int32), axis=1)
    tally = jnp.sum(member)
    before = jnp.cumsum(member) - member
    after = jnp.cumsum(1 - member) - (1 - member)
    place = jnp.where(member == 1, before, tally + after)
    ordering = jnp.zeros_like(member).at[place].set(jnp.arange(member.shape[0], dtype=jnp.int32))
    return (member, place, ordering)


def spread_back(compact, member, place, capacity):
    safe = jnp.minimum(place, capacity - 1)
    return jnp.where(member[:, None] == 1, compact[safe], 0.0)


def shards(x_fwd, act_fwd, ids_fwd, x_bwd, act_bwd, ids_bwd, grad_out, gain, w_router, w_down):
    x_fwd, act_fwd, ids_fwd, x_bwd, act_bwd = (
        x_fwd[0],
        act_fwd[0],
        ids_fwd[0],
        x_bwd[0],
        act_bwd[0],
    )
    ids_bwd, grad_out, gain, w_router, w_down = (
        ids_bwd[0],
        grad_out[0],
        gain[0],
        w_router[0],
        w_down[0],
    )
    experts = w_router.shape[1]
    tokens = ids_fwd.shape[0]
    capacity = tokens // 2
    own_rows = x_fwd.shape[0]
    first_row = lax.axis_index("et") * own_rows
    wide_f, inverse_f, logit_f = norm_logits(x_fwd, gain, w_router)
    backward_wide_rows, backward_inverse_norm, logit_b = norm_logits(x_bwd, gain, w_router)
    full_f, full_b, full_g = (
        lax.all_gather(logit_f, "et", axis=0, tiled=True),
        lax.all_gather(logit_b, "et", axis=0, tiled=True),
        lax.all_gather(grad_out, "et", axis=0, tiled=True),
    )
    route_f, onehot_f, sigma_f, coef_f = routing(full_f, ids_fwd, experts)
    member_f, place_f, order_f = arrange(ids_fwd)
    chosen_f = order_f[:capacity]
    compact = (
        jnp.dot(act_fwd[chosen_f], w_down, preferred_element_type=jnp.float32)
        * coef_f[chosen_f][:, None]
    )
    summed = lax.psum(compact.astype(jnp.bfloat16), "et").astype(jnp.float32)
    member_own = lax.dynamic_slice_in_dim(member_f, first_row, own_rows, 0)
    place_own = lax.dynamic_slice_in_dim(place_f, first_row, own_rows, 0)
    y_mine = spread_back(summed, member_own, place_own, capacity)
    layer_out = (wide_f + y_mine).astype(jnp.bfloat16)
    route_b, onehot_b, sigma_b, backward_coefficient = routing(full_b, ids_bwd, experts)
    member_b, place_b, order_b = arrange(ids_bwd)
    chosen_b = order_b[:capacity]
    up_compact = lax.dot_general(
        full_g[chosen_b], w_down, (((1,), (1,)), ((), ())), preferred_element_type=jnp.float32
    )
    back_up = spread_back(up_compact, member_b, place_b, capacity)
    dact = (backward_coefficient[:, None] * back_up).astype(jnp.bfloat16)
    dprob_part = jnp.sum(act_bwd.astype(jnp.float32) * back_up, axis=1)
    dprob_all = lax.psum(dprob_part, "et")
    dprob_mine = lax.dynamic_slice_in_dim(dprob_all, first_row, own_rows, 0)
    route_mine = lax.dynamic_slice_in_dim(route_b, first_row, own_rows, 0)
    sigma_mine = lax.dynamic_slice_in_dim(sigma_b, first_row, own_rows, 0)
    onehot_mine = lax.dynamic_slice_in_dim(onehot_b, first_row, own_rows, 0)
    slope = route_mine * dprob_mine * sigma_mine * (1.0 - sigma_mine)
    router_wide = w_router.astype(jnp.float32)
    spread = router_wide[:, 0][None, :] - jnp.dot(
        onehot_mine, router_wide.T, precision=lax.Precision.HIGHEST
    )
    dnormed = slope[:, None] * spread
    scaled_rows = dnormed * gain.astype(jnp.float32)
    normalized_input = backward_wide_rows * backward_inverse_norm
    norm_input_gradient = backward_inverse_norm * (
        scaled_rows
        - normalized_input * jnp.mean(scaled_rows * normalized_input, axis=-1, keepdims=True)
    )
    input_grad = (grad_out.astype(jnp.float32) + norm_input_gradient).astype(jnp.bfloat16)
    fwd_in = from_behind(layer_out, "section", 1)
    incoming_gradient = from_behind(input_grad, "section", -1)
    return (fwd_in[None], incoming_gradient[None], dact[None])


def solution(mesh):
    placed = (
        P("section", "et", None),
        P("section", None, "et"),
        P("section", None, None),
        P("section", "et", None),
        P("section", None, "et"),
        P("section", None, None),
        P("section", "et", None),
        P("section", None),
        P("section", None, None),
        P("section", "et", None),
    )
    return jax.shard_map(
        shards,
        mesh=mesh,
        in_specs=placed,
        out_specs=(P("section", "et", None), P("section", "et", None), P("section", None, "et")),
        check_vma=False,
    )
```

profile of v0, /device:TPU:6, one launch (start us, length us, event | category | flops | bytes accessed | tf_op | source)
XLA Modules:
  0.0 256.7 jit_solution(1746351903962819599)
XLA Ops:
  7.2 0.9 convert_reduce_fusion.5
  8.1 1.4 convert_reduce_fusion
  9.5 0.3 reduce-window.34
  9.8 0.1 slice.44
  9.9 0.1 slice_reduce_fusion.3
  10.0 0.3 reduce-window.36
  10.3 0.1 slice.46
  10.4 0.1 slice_reduce_fusion.2
  10.6 0.7 compare_select_fusion.8
  11.3 0.7 compare_select_fusion.2
  11.9 1.4 scatter_custom_fusion
  13.4 0.7 mul.173
  14.1 1.0 fusion.22
  15.1 1.1 fusion.6
  16.3 17.6 %all-gather.1 = bf16[16,16,8]{1,2,0:T(8,128)(2,1)S(1)} all-gather(bf16[1,16,8]{1,2,0:T(8,128)(2,1)S(1)} %fusion.6), channel_id=1, replica_groups=mesh['section'=32,'et'=16] {'et'}, dimensions={0}, use_global_device_ids=true | all-gather | bytes 4352 | tf_op jit(solution)/shard_map/all_gather | solution.py:69
  33.9 0.1 reshape.442
  34.1 1.9 gather_fusion
  36.0 1.3 gather_fusion.1
  37.3 1.5 fusion
  38.8 0.7 all-gather.5.cloned.1.call-update
  39.5 0.1 compare_select_fusion.6
  39.6 0.6 pad_clamp_fusion.2
  40.2 0.1 fusion.26
  40.4 1.0 fusion.7
  41.4 0.3 reduce-window.50
  41.7 0.1 slice.52
  41.8 0.1 slice_reduce_fusion
  41.9 0.1 broadcast_add_fusion
  42.0 0.3 reduce-window.48
  42.3 0.1 slice.50
  42.4 0.1 slice_reduce_fusion.1
  42.6 0.1 broadcast_add_fusion.1
  42.6 1.2 compare_select_fusion
  43.8 1.4 scatter_custom_fusion.1
  45.3 0.7 dynamic-slice_compare_fusion
  45.9 15.0 %all-gather.2 = bf16[16,16,8]{1,2,0:T(8,128)(2,1)S(1)} all-gather(bf16[1,16,8]{1,2,0:T(8,128)(2,1)S(1)} %fusion.7), channel_id=1, replica_groups=mesh['section'=32,'et'=16] {'et'}, dimensions={0}, use_global_device_ids=true | all-gather | bytes 4352 | tf_op jit(solution)/shard_map/all_gather | solution.py:70
  60.9 0.1 reshape.443
  61.0 0.6 pad_clamp_fusion.1
  61.7 0.6 broadcast_compare_fusion.2
  62.2 0.6 iota_compare_fusion
  62.8 0.6 divide_multiply_fusion
  63.4 0.6 add_divide_fusion
  63.9 1.4 slice_convert_fusion
  65.3 92.2 %all-reduce.2.cloned.1.call-done = bf16[128,3072]{1,0:T(8,128)(2,1)} async-done(((bf16[128,3072]{1,0:T(8,128)(2,1)}), bf16[128,3072]{1,0:T(8,128)(2,1)}) %all-reduce.2.cloned.1.call-update) | async-done | bytes 786448 | tf_op jit(solution)/shard_map/psum | solution.py:80
  157.6 2.4 convert_element_type.106
  160.0 2.2 gather_fusion.2
  162.2 0.8 fusion.23
  163.0 3.5 %collective-permute-start = (bf16[16,3072]{1,0:T(8,128)(2,1)S(1)}, bf16[16,3072]{1,0:T(8,128)(2,1)}, u32[]{:S(2)}, u32[]{:S(2)}) collective-permute-start(bf16[16,3072]{1,0:T(8,128)(2,1)S(1)} %fusion.23), channel_id=1, source_target_pairs={{0,16},{16,32},{32,48},{48,64},{64,80},{80,96},{96,112},{112,128},... | collective-permute-start | bytes 294920 | tf_op jit(solution)/shard_map/ppermute | solution.py:10
  166.5 0.6 pad_clamp_fusion
  167.2 2.4 collective-permute-done
  169.6 32.3 %all-gather.5.cloned.1.call-done = bf16[1,256,3072]{2,1,0:T(8,128)(2,1)} async-done(((bf16[1,16,3072]{2,1,0:T(8,128)(2,1)}), bf16[1,256,3072]{2,1,0:T(8,128)(2,1)}) %all-gather.5.cloned.1.call-update) | async-done | bytes 1572880 | tf_op jit(solution)/shard_map/all_gather | solution.py:71
  201.9 4.5 %gather_fusion.3 = bf16[128,3072]{1,0:T(8,128)(2,1)} fusion(bf16[256,3072]{1,0:T(8,128)(2,1)} %bitcast.108, s32[1024]{0:T(1024)} %pad_clamp_fusion.1), kind=kCustom, calls=%fused_computation.3 | custom fusion | bytes 1573376 | tf_op jit(solution)/shard_map/gather | solution.py:89
  206.3 2.3 fusion.3
  208.7 1.8 gather_fusion.4
  210.5 1.3 fusion.8
  211.8 24.9 %psum.15 = f32[256]{0:T(256)S(1)} all-reduce(f32[256]{0:T(256)S(1)} %fusion.8), channel_id=1, replica_groups=mesh['section'=32,'et'=16] {'et'}, use_global_device_ids=true, to_apply=%region_22.23 | all-reduce | flops 256 | bytes 2048 | tf_op jit(solution)/shard_map/psum | solution.py:94
  236.7 0.1 subtract_multiply_fusion
  236.8 1.2 fusion.17
  238.0 1.0 fusion.21
  239.0 2.8 %collective-permute-start.1 = (bf16[16,3072]{1,0:T(8,128)(2,1)S(1)}, bf16[16,3072]{1,0:T(8,128)(2,1)S(1)}, u32[]{:S(2)}, u32[]{:S(2)}) collective-permute-start(bf16[16,3072]{1,0:T(8,128)(2,1)S(1)} %fusion.21), channel_id=1, source_target_pairs={{16,0},{32,16},{48,32},{64,48},{80,64},{96,80},{112,96},{128,112},... | collective-permute-start | bytes 294920 | tf_op jit(solution)/shard_map/ppermute | solution.py:10
  241.8 1.9 fusion.10
  243.7 4.0 %collective-permute-done.1 = bf16[16,3072]{1,0:T(8,128)(2,1)S(1)} collective-permute-done((bf16[16,3072]{1,0:T(8,128)(2,1)S(1)}, bf16[16,3072]{1,0:T(8,128)(2,1)S(1)}, u32[]{:S(2)}, u32[]{:S(2)}) %collective-permute-start.1) | collective-permute-done | bytes 98336 | tf_op jit(solution)/shard_map/ppermute | solution.py:10
  247.6 1.5 copy.20
  249.2 0.6 copy.21
  (47 shorter events, 0.4 us)
Async XLA Ops:
  7.2 30.1 %copy-start = (bf16[1,512,3072]{2,1,0:T(8,128)(2,1)S(1)}, bf16[1,512,3072]{2,1,0:T(8,128)(2,1)}, u32[]{:S(2)}) copy-start(bf16[1,512,3072]{2,1,0:T(8,128)(2,1)} %param.19) | copy-start | bytes 9437188
  7.2 150.4 %all-reduce.2.cloned.1.call-start = ((), (), s32[]{:S(2)}) async-start(), calls=%async_computation | async-start | bytes 1572864 | tf_op jit(solution)/shard_map/psum | solution.py:80
  34.0 6.2 %copy-start.2 = (bf16[1,16,3072]{2,1,0:T(8,128)(2,1)S(1)}, bf16[1,16,3072]{2,1,0:T(8,128)(2,1)}, u32[]{:S(2)}) copy-start(bf16[1,16,3072]{2,1,0:T(8,128)(2,1)} %param.13) | copy-start | bytes 294916
  35.9 25.7 %copy-start.4 = (s32[1,256,2]{1,2,0:T(2,128)S(1)}, s32[1,256,2]{1,2,0:T(2,128)}, u32[]{:S(2)}) copy-start(s32[1,256,2]{1,2,0:T(2,128)} %param.15) | copy-start | bytes 6148
  38.8 123.5 %copy-start.1 = (bf16[1,16,3072]{2,1,0:T(8,128)(2,1)S(1)}, bf16[1,16,3072]{2,1,0:T(8,128)(2,1)}, u32[]{:S(2)}) copy-start(bf16[1,16,3072]{2,1,0:T(8,128)(2,1)} %param.10) | copy-start | bytes 294916
  38.8 163.1 %all-gather.5.cloned.1.call-start = ((), (), s32[]{:S(2)}) async-start(), calls=%async_computation.1 | async-start | bytes 1671168 | tf_op jit(solution)/shard_map/all_gather | solution.py:71
  40.4 1.0 copy-start.9
  163.0 6.6 %collective-permute-start = (bf16[16,3072]{1,0:T(8,128)(2,1)S(1)}, bf16[16,3072]{1,0:T(8,128)(2,1)}, u32[]{:S(2)}, u32[]{:S(2)}) collective-permute-start(bf16[16,3072]{1,0:T(8,128)(2,1)S(1)} %fusion.23), channel_id=1, source_target_pairs={{0,16},{16,32},{32,48},{48,64},{64,80},{80,96},{96,112},{112,128},... | collective-permute-start | bytes 294920 | tf_op jit(solution)/shard_map/ppermute | solution.py:10
  208.7 1.8 copy-start.8
  208.7 28.0 %copy-start.6 = (f32[256]{0:T(256)S(1)}, f32[256]{0:T(256)}, u32[]{:S(2)}) copy-start(f32[256]{0:T(256)} %add_divide_fusion) | copy-start | bytes 3076
  208.7 28.1 %copy-start.3 = (f32[3072,1]{0,1:T(1,128)S(1)}, f32[3072,1]{0,1:T(1,128)}, u32[]{:S(2)}) copy-start(f32[3072,1]{0,1:T(1,128)} %slice_convert_fusion) | copy-start | bytes 36868
  208.7 28.1 %copy-start.7 = (pred[256,8]{0,1:T(8,128)(4,1)S(1)}, pred[256,8]{0,1:T(8,128)(4,1)}, u32[]{:S(2)}) copy-start(pred[256,8]{0,1:T(8,128)(4,1)} %iota_compare_fusion) | copy-start | bytes 6148
  208.7 33.1 %copy-start.5 = (f32[256,1]{0,1:T(1,128)S(1)}, f32[256,1]{0,1:T(1,128)}, u32[]{:S(2)}) copy-start(f32[256,1]{0,1:T(1,128)} %get-tuple-element.14) | copy-start | bytes 3076
  239.0 8.6 %collective-permute-start.1 = (bf16[16,3072]{1,0:T(8,128)(2,1)S(1)}, bf16[16,3072]{1,0:T(8,128)(2,1)S(1)}, u32[]{:S(2)}, u32[]{:S(2)}) collective-permute-start(bf16[16,3072]{1,0:T(8,128)(2,1)S(1)} %fusion.21), channel_id=1, source_target_pairs={{16,0},{32,16},{48,32},{64,48},{80,64},{96,80},{112,96},{128,112},... | collective-permute-start | bytes 294920 | tf_op jit(solution)/shard_map/ppermute | solution.py:10
Sparse Core Ops, SparseCore 0:
  38.9 118.5 all-reduce.1
  159.7 42.1 all-gather.4
where the time goes:
time: 257 us
  waiting for transfers between devices  132 us (51%)
  blocking collectives  57.5 us (22%)
  other arithmetic  22.1 us (9%)
  local copies, waits for them, and re-layouts  17.6 us (7%)
  between operations  14.3 us (6%)
  matrix products  7.15 us (3%)
  starting transfers between devices  6.38 us (2%)
    psum x1, waiting for transfers between devices, shards(): summed = lax.psum(compact.astype(jnp.bfloat16), 'et').astype(jnp.float32)  92.2 us
    all_gather x1, waiting for transfers between devices, shards(): lax.all_gather(grad_out, 'et', axis=0, tiled=True)  32.3 us
    psum x1, blocking collectives, shards(): dprob_all = lax.psum(dprob_part, 'et')  24.9 us
    all_gather x1, blocking collectives, shards(): lax.all_gather(logit_f, 'et', axis=0, tiled=True)  17.6 us
    all_gather x1, blocking collectives, shards(): lax.all_gather(logit_b, 'et', axis=0, tiled=True)  15 us
    ppermute x2, waiting for transfers between devices, from_behind(): lax.ppermute(value, axis, [(source, source + steps) for source in range(f...  6.38 us
    ppermute x2, starting transfers between devices, from_behind(): lax.ppermute(value, axis, [(source, source + steps) for source in range(f...  6.3 us
  transfers between devices with their start and end apart: 4, of which 4 were waited for; matrix products, arithmetic and copies ran while one was open for 7% of the time, Pallas kernels for 0%

commit v1 on v0

--- a/solution.py
+++ b/solution.py
@@ -91,7 +91,8 @@
     back_up = spread_back(up_compact, member_b, place_b, capacity)
     dact = (backward_coefficient[:, None] * back_up).astype(jnp.bfloat16)
     dprob_part = jnp.sum(act_bwd.astype(jnp.float32) * back_up, axis=1)
-    dprob_all = lax.psum(dprob_part, "et")
+    parts = lax.all_gather(dprob_part, "et", axis=0, tiled=False)
+    dprob_all = parts.sum(axis=0)
     dprob_mine = lax.dynamic_slice_in_dim(dprob_all, first_row, own_rows, 0)
     route_mine = lax.dynamic_slice_in_dim(route_b, first_row, own_rows, 0)
     sigma_mine = lax.dynamic_slice_in_dim(sigma_b, first_row, own_rows, 0)

time: 257 us -> 249 us (0.969)
  blocking collectives: 57.5 us -> 48.3 us
    psum x1 -> x0, blocking collectives: 24.9 us -> none  [shards(): dprob_all = lax.psum(dprob_part, 'et')]
    all_gather x0 -> x1, blocking collectives: none -> 15.7 us  [shards(): parts = lax.all_gather(dprob_part, 'et', axis=0, tiled=False)]
  transfers between devices with their start and end apart: 4 -> 4, of which waited for: 4 -> 4; matrix products, arithmetic and copies ran while one was open for 7% -> 8% of each run, Pallas kernels for 0% -> 0%
where the time goes in v1:
time: 249 us; the launch traced here: 248 us
  waiting for transfers between devices  132 us (53%)
  blocking collectives  48.3 us (19%)
  other arithmetic  22.2 us (9%)
  local copies, waits for them, and re-layouts  17.6 us (7%)
  between operations  14.3 us (6%)
  matrix products  7.15 us (3%)
  starting transfers between devices  6.38 us (3%)
    psum x1, waiting for transfers between devices, shards(): summed = lax.psum(compact.astype(jnp.bfloat16), 'et').astype(jnp.float32)  92.2 us
    all_gather x1, waiting for transfers between devices, shards(): lax.all_gather(grad_out, 'et', axis=0, tiled=True)  32.3 us
    all_gather x1, blocking collectives, shards(): lax.all_gather(logit_f, 'et', axis=0, tiled=True)  17.6 us
    all_gather x1, blocking collectives, shards(): parts = lax.all_gather(dprob_part, 'et', axis=0, tiled=False)  15.7 us
    all_gather x1, blocking collectives, shards(): lax.all_gather(logit_b, 'et', axis=0, tiled=True)  15 us
    ppermute x2, waiting for transfers between devices, from_behind(): lax.ppermute(value, axis, [(source, source + steps) for source in range(f...  6.82 us
    ppermute x2, starting transfers between devices, from_behind(): lax.ppermute(value, axis, [(source, source + steps) for source in range(f...  6.3 us
  transfers between devices with their start and end apart: 4, of which 4 were waited for; matrix products, arithmetic and copies ran while one was open for 8% of the time, Pallas kernels for 0%

profile of v1, /device:TPU:6, one launch (start us, length us, event | category | flops | bytes accessed | tf_op | source)
XLA Modules:
  0.0 247.9 jit_solution(7735916414955716565)
XLA Ops:
  7.2 0.9 convert_reduce_fusion.5
  8.1 1.4 convert_reduce_fusion
  9.5 0.3 reduce-window.34
  9.8 0.1 slice.44
  9.9 0.1 slice_reduce_fusion.3
  10.0 0.3 reduce-window.36
  10.3 0.1 slice.46
  10.4 0.1 slice_reduce_fusion.2
  10.6 0.7 compare_select_fusion.8
  11.3 0.7 compare_select_fusion.2
  11.9 1.4 scatter_custom_fusion
  13.4 0.7 mul.173
  14.1 1.0 fusion.22
  15.1 1.1 fusion.6
  16.3 17.6 %all-gather.2 = bf16[16,16,8]{1,2,0:T(8,128)(2,1)S(1)} all-gather(bf16[1,16,8]{1,2,0:T(8,128)(2,1)S(1)} %fusion.6), channel_id=1, replica_groups=mesh['section'=32,'et'=16] {'et'}, dimensions={0}, use_global_device_ids=true | all-gather | bytes 4352 | tf_op jit(solution)/shard_map/all_gather | solution.py:69
  33.9 0.1 reshape.445
  34.1 1.9 gather_fusion
  36.0 1.3 gather_fusion.1
  37.3 1.5 fusion
  38.8 0.7 all-gather.7.cloned.1.call-update
  39.5 0.1 compare_select_fusion.6
  39.6 0.6 pad_clamp_fusion.2
  40.2 0.1 fusion.26
  40.4 1.0 fusion.7
  41.4 0.3 reduce-window.50
  41.7 0.1 slice.52
  41.8 0.1 slice_reduce_fusion
  41.9 0.1 broadcast_add_fusion
  42.0 0.3 reduce-window.48
  42.3 0.1 slice.50
  42.4 0.1 slice_reduce_fusion.1
  42.6 0.1 broadcast_add_fusion.1
  42.6 1.2 compare_select_fusion
  43.8 1.4 scatter_custom_fusion.1
  45.3 0.7 dynamic-slice_compare_fusion
  45.9 15.0 %all-gather.4 = bf16[16,16,8]{1,2,0:T(8,128)(2,1)S(1)} all-gather(bf16[1,16,8]{1,2,0:T(8,128)(2,1)S(1)} %fusion.7), channel_id=1, replica_groups=mesh['section'=32,'et'=16] {'et'}, dimensions={0}, use_global_device_ids=true | all-gather | bytes 4352 | tf_op jit(solution)/shard_map/all_gather | solution.py:70
  60.9 0.1 reshape.446
  61.0 0.6 pad_clamp_fusion.1
  61.7 0.6 broadcast_compare_fusion.2
  62.2 0.6 iota_compare_fusion
  62.8 0.6 divide_multiply_fusion
  63.4 0.6 add_divide_fusion
  63.9 1.4 slice_convert_fusion
  65.3 92.2 %all-reduce.2.cloned.1.call-done = bf16[128,3072]{1,0:T(8,128)(2,1)} async-done(((bf16[128,3072]{1,0:T(8,128)(2,1)}), bf16[128,3072]{1,0:T(8,128)(2,1)}) %all-reduce.2.cloned.1.call-update) | async-done | bytes 786448 | tf_op jit(solution)/shard_map/psum | solution.py:80
  157.6 2.4 convert_element_type.106
  160.0 2.2 gather_fusion.2
  162.2 0.8 fusion.23
  163.0 3.5 %collective-permute-start = (bf16[16,3072]{1,0:T(8,128)(2,1)S(1)}, bf16[16,3072]{1,0:T(8,128)(2,1)}, u32[]{:S(2)}, u32[]{:S(2)}) collective-permute-start(bf16[16,3072]{1,0:T(8,128)(2,1)S(1)} %fusion.23), channel_id=1, source_target_pairs={{0,16},{16,32},{32,48},{48,64},{64,80},{80,96},{96,112},{112,128},... | collective-permute-start | bytes 294920 | tf_op jit(solution)/shard_map/ppermute | solution.py:10
  166.5 0.6 pad_clamp_fusion
  167.2 2.4 collective-permute-done
  169.6 32.3 %all-gather.7.cloned.1.call-done = bf16[1,256,3072]{2,1,0:T(8,128)(2,1)} async-done(((bf16[1,16,3072]{2,1,0:T(8,128)(2,1)}), bf16[1,256,3072]{2,1,0:T(8,128)(2,1)}) %all-gather.7.cloned.1.call-update) | async-done | bytes 1572880 | tf_op jit(solution)/shard_map/all_gather | solution.py:71
  201.9 4.5 %gather_fusion.3 = bf16[128,3072]{1,0:T(8,128)(2,1)} fusion(bf16[256,3072]{1,0:T(8,128)(2,1)} %bitcast.109, s32[1024]{0:T(1024)} %pad_clamp_fusion.1), kind=kCustom, calls=%fused_computation.3 | custom fusion | bytes 1573376 | tf_op jit(solution)/shard_map/gather | solution.py:89
  206.3 2.3 fusion.3
  208.7 1.8 gather_fusion.4
  210.5 1.3 fusion.8
  211.8 15.7 %all-gather.3 = f32[16,1,256]{2,1,0:T(1,128)S(1)} all-gather(f32[1,1,256]{2,1,0:T(1,128)S(1)} %bitcast.123), channel_id=3, replica_groups=mesh['section'=32,'et'=16] {'et'}, dimensions={0}, use_global_device_ids=true | all-gather | bytes 17408 | tf_op jit(solution)/shard_map/all_gather | solution.py:94
  227.5 0.1 subtract_multiply_fusion
  227.6 1.2 fusion.17
  228.8 1.0 fusion.21
  229.8 2.8 %collective-permute-start.1 = (bf16[16,3072]{1,0:T(8,128)(2,1)S(1)}, bf16[16,3072]{1,0:T(8,128)(2,1)S(1)}, u32[]{:S(2)}, u32[]{:S(2)}) collective-permute-start(bf16[16,3072]{1,0:T(8,128)(2,1)S(1)} %fusion.21), channel_id=1, source_target_pairs={{16,0},{32,16},{48,32},{64,48},{80,64},{96,80},{112,96},{128,112},... | collective-permute-start | bytes 294920 | tf_op jit(solution)/shard_map/ppermute | solution.py:10
  232.6 1.9 fusion.10
  234.5 4.4 %collective-permute-done.1 = bf16[16,3072]{1,0:T(8,128)(2,1)S(1)} collective-permute-done((bf16[16,3072]{1,0:T(8,128)(2,1)S(1)}, bf16[16,3072]{1,0:T(8,128)(2,1)S(1)}, u32[]{:S(2)}, u32[]{:S(2)}) %collective-permute-start.1) | collective-permute-done | bytes 98336 | tf_op jit(solution)/shard_map/ppermute | solution.py:10
  238.9 1.5 copy.20
  240.4 0.6 copy.21
  (48 shorter events, 0.5 us)
Async XLA Ops:
  7.2 30.1 %copy-start = (bf16[1,512,3072]{2,1,0:T(8,128)(2,1)S(1)}, bf16[1,512,3072]{2,1,0:T(8,128)(2,1)}, u32[]{:S(2)}) copy-start(bf16[1,512,3072]{2,1,0:T(8,128)(2,1)} %param.19) | copy-start | bytes 9437188
  7.2 150.4 %all-reduce.2.cloned.1.call-start = ((), (), s32[]{:S(2)}) async-start(), calls=%async_computation | async-start | bytes 1572864 | tf_op jit(solution)/shard_map/psum | solution.py:80
  34.0 6.2 %copy-start.2 = (bf16[1,16,3072]{2,1,0:T(8,128)(2,1)S(1)}, bf16[1,16,3072]{2,1,0:T(8,128)(2,1)}, u32[]{:S(2)}) copy-start(bf16[1,16,3072]{2,1,0:T(8,128)(2,1)} %param.13) | copy-start | bytes 294916
  35.9 25.7 %copy-start.4 = (s32[1,256,2]{1,2,0:T(2,128)S(1)}, s32[1,256,2]{1,2,0:T(2,128)}, u32[]{:S(2)}) copy-start(s32[1,256,2]{1,2,0:T(2,128)} %param.15) | copy-start | bytes 6148
  38.8 123.5 %copy-start.1 = (bf16[1,16,3072]{2,1,0:T(8,128)(2,1)S(1)}, bf16[1,16,3072]{2,1,0:T(8,128)(2,1)}, u32[]{:S(2)}) copy-start(bf16[1,16,3072]{2,1,0:T(8,128)(2,1)} %param.10) | copy-start | bytes 294916
  38.8 163.1 %all-gather.7.cloned.1.call-start = ((), (), s32[]{:S(2)}) async-start(), calls=%async_computation.1 | async-start | bytes 1671168 | tf_op jit(solution)/shard_map/all_gather | solution.py:71
  40.4 1.0 copy-start.9
  163.0 6.6 %collective-permute-start = (bf16[16,3072]{1,0:T(8,128)(2,1)S(1)}, bf16[16,3072]{1,0:T(8,128)(2,1)}, u32[]{:S(2)}, u32[]{:S(2)}) collective-permute-start(bf16[16,3072]{1,0:T(8,128)(2,1)S(1)} %fusion.23), channel_id=1, source_target_pairs={{0,16},{16,32},{32,48},{48,64},{64,80},{80,96},{96,112},{112,128},... | collective-permute-start | bytes 294920 | tf_op jit(solution)/shard_map/ppermute | solution.py:10
  208.7 1.8 copy-start.8
  208.7 18.9 %copy-start.6 = (f32[256]{0:T(256)S(1)}, f32[256]{0:T(256)}, u32[]{:S(2)}) copy-start(f32[256]{0:T(256)} %add_divide_fusion) | copy-start | bytes 3076
  208.7 18.9 %copy-start.3 = (f32[3072,1]{0,1:T(1,128)S(1)}, f32[3072,1]{0,1:T(1,128)}, u32[]{:S(2)}) copy-start(f32[3072,1]{0,1:T(1,128)} %slice_convert_fusion) | copy-start | bytes 36868
  208.7 18.9 %copy-start.7 = (pred[256,8]{0,1:T(8,128)(4,1)S(1)}, pred[256,8]{0,1:T(8,128)(4,1)}, u32[]{:S(2)}) copy-start(pred[256,8]{0,1:T(8,128)(4,1)} %iota_compare_fusion) | copy-start | bytes 6148
  208.7 23.9 %copy-start.5 = (f32[256,1]{0,1:T(1,128)S(1)}, f32[256,1]{0,1:T(1,128)}, u32[]{:S(2)}) copy-start(f32[256,1]{0,1:T(1,128)} %get-tuple-element.14) | copy-start | bytes 3076
  229.8 9.0 %collective-permute-start.1 = (bf16[16,3072]{1,0:T(8,128)(2,1)S(1)}, bf16[16,3072]{1,0:T(8,128)(2,1)S(1)}, u32[]{:S(2)}, u32[]{:S(2)}) collective-permute-start(bf16[16,3072]{1,0:T(8,128)(2,1)S(1)} %fusion.21), channel_id=1, source_target_pairs={{16,0},{32,16},{48,32},{64,48},{80,64},{96,80},{112,96},{128,112},... | collective-permute-start | bytes 294920 | tf_op jit(solution)/shard_map/ppermute | solution.py:10
Sparse Core Ops, SparseCore 0:
  38.9 118.5 all-reduce.1
  159.7 42.1 all-gather.6
